TPU v7x, 32 devices: a whole 2x2x4 slice. The times are simulated.
32 devices in a mesh: seq: 8 (over y, x, core), chan: 4 (over z).
Axes of the slice: x: 2, y: 2, z: 4, core: 2. Of those that a mesh axis runs over, the one named last changes fastest.
Arguments:
- query_proj: bfloat16 [1024, 8192], P('seq', 'chan'), may hold values from -8 to 8
- key_proj: bfloat16 [1024, 8192], P('seq', 'chan'), may hold values from -8 to 8
- value_proj: bfloat16 [1024, 8192], P('seq', 'chan'), may hold values from -6 to 6
- residual: bfloat16 [1024, 8192], P('seq', 'chan'), may hold values from -6 to 6
- out_weight: bfloat16 [8192, 8192], P('chan', 'seq'), may hold values from -0.0625 to 0.0625
Outputs:
- attn_out: bfloat16 [1024, 8192], P('seq', 'chan')
All inputs are finite; a program needn't handle non-finite values.
Results may differ from a plain program's by a relative error of at most 0.008.
Values may be sent and summed in bfloat16 or wider, within the bound.
No kernel may reach another device: no remote copies, remote signals or barrier semaphores. Data moves between devices by JAX's collectives and lax.ppermute only.
A program may use at most 64 MiB of HBM per device.

v0:
```python
import math
import jax
import jax.numpy as jnp
from jax import lax
from jax.sharding import PartitionSpec as P

HEAD_DIM = 128


def attend(state, query_rows, first_pos, key_block, value_block, block_start, score_scale):
    row_max, row_total, accum = state
    scores = (
        jnp.einsum("qhd,khd->hqk", query_rows, key_block, preferred_element_type=jnp.float32)
        * score_scale
    )
    row_pos = first_pos + jnp.arange(query_rows.shape[0], dtype=jnp.int32)
    col_pos = block_start + jnp.arange(key_block.shape[0], dtype=jnp.int32)
    allowed = (col_pos[None, :] <= row_pos[:, None])[None]
    scores = jnp.where(allowed, scores, -1e30)
    new_max = jnp.maximum(row_max, jnp.max(scores, axis=-1))
    weights = jnp.where(allowed, jnp.exp(scores - new_max[..., None]), 0.0)
    factor = jnp.exp(row_max - new_max)
    row_total = row_total * factor + jnp.sum(weights, axis=-1)
    accum = accum * factor[..., None] + jnp.einsum(
        "hqk,khd->hqd",
        weights.astype(jnp.bfloat16),
        value_block,
        preferred_element_type=jnp.float32,
    )
    return (new_max, row_total, accum)


def guarded(state, query_rows, first_pos, key_block, value_block, block_start, score_scale):
    last_pos = first_pos + query_rows.shape[0] - 1

    def do_update(inner):
        return attend(
            inner, query_rows, first_pos, key_block, value_block, block_start, score_scale
        )

    def keep_state(inner):
        return inner

    return lax.cond(block_start <= last_pos, do_update, keep_state, state)


def per_device(query_proj, key_proj, value_proj, residual, out_weight):
    seg_rows = query_proj.shape[0]
    feat_width = query_proj.shape[1]
    heads_here = feat_width // HEAD_DIM
    seq_count = lax.axis_size("seq")
    chan_count = lax.axis_size("chan")
    segment = lax.axis_index("seq")
    score_scale = 1.0 / math.sqrt(HEAD_DIM)
    groups = [(query_proj, segment * seg_rows)]
    shaped = [
        (rows.reshape(rows.shape[0], heads_here, HEAD_DIM), first_pos) for rows, first_pos in groups
    ]
    starting = tuple(
        (
            (
                jnp.full((heads_here, rows.shape[0]), -1e30, jnp.float32),
                jnp.zeros((heads_here, rows.shape[0]), jnp.float32),
                jnp.zeros((heads_here, rows.shape[0], HEAD_DIM), jnp.float32),
            )
            for rows, first_pos in shaped
        )
    )
    piece_keys = lax.all_gather(key_proj, "seq", axis=0, tiled=True)
    piece_values = lax.all_gather(value_proj, "seq", axis=0, tiled=True)
    piece_rows = piece_keys.shape[0]

    def one_block(block_index, states):
        offset = block_index * seg_rows
        key_block = lax.dynamic_slice_in_dim(piece_keys, offset, seg_rows, 0).reshape(
            seg_rows, heads_here, HEAD_DIM
        )
        value_block = lax.dynamic_slice_in_dim(piece_values, offset, seg_rows, 0).reshape(
            seg_rows, heads_here, HEAD_DIM
        )
        updated = []
        for (query_rows, first_pos), state in zip(shaped, states):
            updated.append(
                guarded(state, query_rows, first_pos, key_block, value_block, offset, score_scale)
            )
        return tuple(updated)

    finals = lax.fori_loop(0, piece_rows // seg_rows, one_block, starting)
    pieces_out = []
    for row_max, row_total, accum in finals:
        ratio = accum / row_total[..., None]
        pieces_out.append(
            ratio.transpose(1, 0, 2).reshape(ratio.shape[1], feat_width).astype(jnp.bfloat16)
        )
    local_context = pieces_out[0]
    gathered = lax.all_gather(local_context, "seq", axis=0, tiled=True)
    sub_rows = seg_rows // chan_count
    grid = gathered.reshape(seq_count, chan_count, sub_rows, feat_width)
    block_tokens = seq_count * sub_rows
    rows = grid.transpose(1, 0, 2, 3).reshape(block_tokens * lax.axis_size("chan"), feat_width)
    partial_sums = lax.psum_scatter(
        jnp.dot(rows, out_weight, preferred_element_type=jnp.float32).astype(jnp.bfloat16),
        "chan",
        scatter_dimension=0,
        tiled=True,
    ).astype(jnp.float32)
    relaid = lax.all_to_all(
        lax.all_to_all(
            partial_sums.astype(jnp.bfloat16), "seq", split_axis=0, concat_axis=1, tiled=True
        ),
        "chan",
        split_axis=1,
        concat_axis=0,
        tiled=True,
    ).astype(partial_sums.dtype)
    return (residual.astype(jnp.float32) + relaid).astype(jnp.bfloat16)


def solution(mesh):
    placed = (
        P("seq", "chan"),
        P("seq", "chan"),
        P("seq", "chan"),
        P("seq", "chan"),
        P("chan", "seq"),
    )
    return jax.shard_map(
        per_device, mesh=mesh, in_specs=placed, out_specs=P("seq", "chan"), check_vma=False
    )
```

profile of v0, /device:TPU:0, one launch (start us, length us, event | category | flops | bytes accessed | tf_op | source)
XLA Modules:
  0.0 250.2 jit_solution(13693621716920695424)
XLA Ops:
  6.5 2.0 copy.32
  8.6 0.0 all-gather.6.cloned.1.call-start
  8.7 2.1 copy.34
  10.7 0.0 all-gather.6.cloned.1.call-update
  10.8 0.0 all-gather.8.cloned.1.call-start
  10.8 1.3 copy.33
  12.1 0.3 copy.35
  12.4 37.0 %all-gather.4.cloned.1.call-done = bf16[1024,2048]{0,1:T(8,128)(2,1)} async-done(((bf16[128,2048]{0,1:T(8,128)(2,1)}), bf16[1024,2048]{0,1:T(8,128)(2,1)}) %all-gather.4.cloned.1.call-update) | async-done | bytes 4194320 | tf_op jit(solution)/shard_map/all_gather | solution.py:69
  49.4 39.3 %all-gather.6.cloned.1.call-done = bf16[1024,2048]{0,1:T(8,128)(2,1)} async-done(((bf16[128,2048]{0,1:T(8,128)(2,1)}), bf16[1024,2048]{0,1:T(8,128)(2,1)}) %all-gather.6.cloned.1.call-update) | async-done | bytes 4194320 | tf_op jit(solution)/shard_map/all_gather | solution.py:70
  88.8 0.1 broadcast_in_dim.45
  88.9 3.3 %while.19 = (s32[]{:T(128)}, f32[16,128]{1,0:T(8,128)S(1)}, f32[16,128]{1,0:T(8,128)S(1)}, f32[16,128,128]{2,1,0:T(8,128)S(1)}, s32[]{:T(128)}, /*index=5*/s32[]...) while((s32[]{:T(128)}, f32[16,128]{1,0:T(8,128)S(1)}, ...), condition=%wide.region_5.6_spmd, body=%wide.region_0.5_spmd.sunk | while | flops 137122048 | bytes 9111853 | solution.py:88
  88.9 3.0 %conditional.2 = ((f32[16,128]{1,0:T(8,128)S(1)}, f32[16,128]{1,0:T(8,128)S(1)}, f32[16,128,128]{2,1,0:T(8,128)S(1)})) conditional(s32[]{:T(128)} %convert_element_type.63, (f32[16,128]{1,0:T(8,128)S(1)}, f32[16,128]{1,0:T(8,128)S(1)}, f32[16,128,128]{2,1,0:T(8,128)S(1)}) %tuple.61, (s32[]{:T(128)}, s32[]{:T(128)}, bf16[1024,2048]{0,1:T(8,128)(2,1)}, ...), branch_computations={%region_1.0_spmd, %region_2.4_spmd} | conditional | flops 137122048 | bytes 9111630 | solution.py:44
  88.9 1.3 constant_dynamic-slice_fusion
  90.2 0.1 broadcast_compare_fusion
  90.3 0.5 fusion.10
  90.8 0.2 fusion.3
  91.1 0.8 convolution_add_fusion
  92.2 0.3 copy.36
  92.5 0.9 divide_convert_fusion
  93.5 0.0 reduce-scatter.2.cloned.1.call-start
  93.5 58.4 %all-gather.8.cloned.1.call-done = bf16[1024,2048]{0,1:T(8,128)(2,1)} async-done(((bf16[128,2048]{0,1:T(8,128)(2,1)}), bf16[1024,2048]{0,1:T(8,128)(2,1)}) %all-gather.8.cloned.1.call-update) | async-done | bytes 4194320 | tf_op jit(solution)/shard_map/all_gather | solution.py:96
  151.9 6.5 %copy.37 = bf16[1024,2048]{1,0:T(8,128)(2,1)} copy(bf16[1024,2048]{0,1:T(8,128)(2,1)} %all-gather.8.cloned.1.call-done) | data formatting | bytes 8388608 | tf_op jit(solution)/shard_map/all_gather | solution.py:96
  158.4 2.7 %copy.38 = bf16[4,8,32,2048]{3,2,1,0:T(8,128)(2,1)S(1)} copy(bf16[4,8,32,2048]{3,2,0,1:T(8,128)(2,1)} %bitcast.29) | data formatting | bytes 8388608 | tf_op jit(solution)/shard_map/transpose | solution.py:100
  161.1 0.8 copy-done.1
  161.9 5.7 %convolution_convert_fusion = bf16[1024,1024]{1,0:T(8,128)(2,1)} fusion(bf16[1024,2048]{1,0:T(8,128)(2,1)S(1)} %bitcast.30, bf16[2048,1024]{1,0:T(8,128)(2,1)S(1)} %copy-done.1), kind=kOutput, calls=%fused_computation.18 | convolution fusion | flops 4296015872 | bytes 10485760 | tf_op jit(solution)/shard_map/dot_general | solution.py:102
  167.7 44.0 %reduce-scatter.2.cloned.1.call-done = bf16[256,1024]{1,0:T(8,128)(2,1)} async-done(((bf16[1024,1024]{1,0:T(8,128)(2,1)}), bf16[256,1024]{1,0:T(8,128)(2,1)}) %reduce-scatter.2.cloned.1.call-update) | async-done | bytes 524304 | tf_op jit(solution)/shard_map/reduce_scatter | solution.py:101
  211.7 13.4 %all_to_all.29 = bf16[8,32,1024]{2,1,0:T(8,128)(2,1)S(1)} all-to-all(bf16[8,32,1024]{2,1,0:T(8,128)(2,1)} %bitcast.34), channel_id=1, replica_groups=mesh['seq'=8,'chan'=4] {'seq'}, dimensions={0} | all-to-all | bytes 1048576 | tf_op jit(solution)/shard_map/all_to_all | solution.py:108
  225.1 0.3 copy.39
  225.3 0.4 all_to_all.25
  225.7 0.3 copy.40
  226.0 16.7 %all_to_all.30 = bf16[32,4,2048]{2,0,1:T(8,128)(2,1)S(1)} all-to-all(bf16[32,4,2048]{2,0,1:T(8,128)(2,1)S(1)} %copy.40), channel_id=1, replica_groups=mesh['seq'=8,'chan'=4] {'chan'}, dimensions={1} | all-to-all | bytes 1048576 | tf_op jit(solution)/shard_map/all_to_all | solution.py:107
  242.7 0.9 fusion.9
  (20 shorter events, 0.2 us)
Async XLA Ops:
  6.5 42.9 %all-gather.4.cloned.1.call-start = ((), (), s32[]{:S(2)}) async-start(), calls=%async_computation.3 | async-start | bytes 4718592 | tf_op jit(solution)/shard_map/all_gather | solution.py:69
  8.6 80.1 %all-gather.6.cloned.1.call-start = ((), (), s32[]{:S(2)}) async-start(), calls=%async_computation.4 | async-start | bytes 4718592 | tf_op jit(solution)/shard_map/all_gather | solution.py:70
  10.8 141.2 %all-gather.8.cloned.1.call-start = ((), (), s32[]{:S(2)}) async-start(), calls=%async_computation.5 | async-start | bytes 4718592 | tf_op jit(solution)/shard_map/all_gather | solution.py:96
  93.5 118.2 %reduce-scatter.2.cloned.1.call-start = ((), (), s32[]{:S(2)}) async-start(), calls=%async_computation.6 | async-start | bytes 2621440 | tf_op jit(solution)/shard_map/reduce_scatter | solution.py:101
  158.4 3.4 %copy-start.1 = (bf16[2048,1024]{1,0:T(8,128)(2,1)S(1)}, bf16[2048,1024]{1,0:T(8,128)(2,1)}, u32[]{:S(2)}) copy-start(bf16[2048,1024]{1,0:T(8,128)(2,1)} %param.13) | copy-start | bytes 12582916
  167.6 75.1 %copy-start = (bf16[128,2048]{1,0:T(8,128)(2,1)S(1)}, bf16[128,2048]{1,0:T(8,128)(2,1)}, u32[]{:S(2)}) copy-start(bf16[128,2048]{1,0:T(8,128)(2,1)} %param.12) | copy-start | bytes 1572868
Sparse Core Ops, SparseCore 0:
  9.2 40.1 all-gather.3
  51.3 37.4 all-gather.5
  93.6 58.2 all-gather.7
  167.8 43.8 reduce-scatter.1
where the time goes:
time: 251 us; the launch traced here: 250 us
  waiting for transfers between devices  179 us (71%)
  blocking collectives  30.1 us (12%)
  local copies, waits for them, and re-layouts  18.4 us (7%)
  between operations  13.2 us (5%)
  matrix products  7.06 us (3%)
    all_gather x1, waiting for transfers between devices, per_device(): gathered = lax.all_gather(local_context, 'seq', axis=0, tiled=True)  58.4 us
    reduce_scatter x1, waiting for transfers between devices, per_device(): lax.psum_scatter(jnp.dot(rows, out_weight, preferred_element_type=jnp.flo...  44 us
    all_gather x1, waiting for transfers between devices, per_device(): piece_values = lax.all_gather(value_proj, 'seq', axis=0, tiled=True)  39.3 us
    all_gather x1, waiting for transfers between devices, per_device(): piece_keys = lax.all_gather(key_proj, 'seq', axis=0, tiled=True)  37 us
    all_to_all x1, blocking collectives, per_device(): lax.all_to_all(lax.all_to_all(partial_sums.astype(jnp.bfloat16), 'seq', s...  16.7 us
    all_to_all x1, blocking collectives, per_device(): lax.all_to_all(partial_sums.astype(jnp.bfloat16), 'seq', split_axis=0, co...  13.4 us
    all_gather x1, local copies, waits for them, and re-layouts, per_device(): gathered = lax.all_gather(local_context, 'seq', axis=0, tiled=True)  6.53 us
    unnamed x7, local copies, waits for them, and re-layouts  6.22 us
  transfers between devices with their start and end apart: 4, of which 4 were waited for; matrix products, arithmetic and copies ran while one was open for 1% of the time, Pallas kernels for 0%

commit v1 on v0

--- a/solution.py
+++ b/solution.py
@@ -67,7 +67,25 @@
         )
     )
     piece_keys = lax.all_gather(key_proj, "seq", axis=0, tiled=True)
-    piece_values = lax.all_gather(value_proj, "seq", axis=0, tiled=True)
+    size, place, span = (lax.axis_size("seq"), lax.axis_index("seq"), value_proj.shape[0])
+    ahead = [(i, (i + 1) % size) for i in range(size)]
+    downward = [(i, (i - 1) % size) for i in range(size)]
+    piece_values = jnp.zeros(
+        (*value_proj.shape[:0], size * span, *value_proj.shape[0 + 1 :]), value_proj.dtype
+    )
+    piece_values = lax.dynamic_update_slice_in_dim(piece_values, value_proj, place * span, axis=0)
+    from_left = from_right = value_proj
+    half = size // 2
+    for step in range(1, half + 1):
+        from_left = lax.ppermute(from_left, "seq", ahead)
+        piece_values = lax.dynamic_update_slice_in_dim(
+            piece_values, from_left, (place - step) % size * span, axis=0
+        )
+        if step < size - half:
+            from_right = lax.ppermute(from_right, "seq", downward)
+            piece_values = lax.dynamic_update_slice_in_dim(
+                piece_values, from_right, (place + step) % size * span, axis=0
+            )
     piece_rows = piece_keys.shape[0]
 
     def one_block(block_index, states):

time: 251 us -> 234 us (0.932)
  waiting for transfers between devices: 179 us -> 139 us
  starting transfers between devices: 0.13 us -> 13.4 us
  local copies, waits for them, and re-layouts: 18.4 us -> 27.4 us
    all_gather x1 -> x0, waiting for transfers between devices: 39.3 us -> none  [per_device(): piece_values = lax.all_gather(value_proj, 'seq', axis=0, tiled=True)]
    ppermute x0 -> x7, waiting for transfers between devices: none -> 38.2 us  [the longest x4 23.6 us: per_device(): from_left = lax.ppermute(from_left, 'seq', ahead)]
    all_gather x1, waiting for transfers between devices: 37 us -> 0.01 us  [per_device(): piece_keys = lax.all_gather(key_proj, 'seq', axis=0, tiled=True)]
    ppermute x0 -> x7, starting transfers between devices: none -> 13.4 us  [the longest x3 8.66 us: per_device(): from_right = lax.ppermute(from_right, 'seq', downward)]
    dynamic_update_slice x0 -> x8, local copies, waits for them, and re-layouts: none -> 8.21 us  [the longest x3 3.73 us: per_device(): lax.dynamic_update_slice_in_dim(piece_values, from_right, (place + step)...]
    broadcast_in_dim x0 -> x1, local copies, waits for them, and re-layouts: none -> 2.52 us  [per_device(): jnp.zeros((*value_proj.shape[:0], size * span, *value_proj.shape[0 + 1:])...]
    unnamed x7 -> x9, local copies, waits for them, and re-layouts: 6.22 us -> 4.47 us
  transfers between devices with their start and end apart: 4 -> 10, of which waited for: 4 -> 8; matrix products, arithmetic and copies ran while one was open for 1% -> 5% of each run, Pallas kernels for 0% -> 0%
where the time goes in v1:
time: 234 us; the launch traced here: 233 us
  waiting for transfers between devices  139 us (59%)
  blocking collectives  30.1 us (13%)
  local copies, waits for them, and re-layouts  27.4 us (12%)
  starting transfers between devices  13.4 us (6%)
  between operations  13.2 us (6%)
  matrix products  7.08 us (3%)
    all_gather x1, waiting for transfers between devices, per_device(): gathered = lax.all_gather(local_context, 'seq', axis=0, tiled=True)  57 us
    reduce_scatter x1, waiting for transfers between devices, per_device(): lax.psum_scatter(jnp.dot(rows, out_weight, preferred_element_type=jnp.flo...  44 us
    ppermute x4, waiting for transfers between devices, per_device(): from_left = lax.ppermute(from_left, 'seq', ahead)  23.6 us
    all_to_all x1, blocking collectives, per_device(): lax.all_to_all(lax.all_to_all(partial_sums.astype(jnp.bfloat16), 'seq', s...  16.7 us
    ppermute x3, waiting for transfers between devices, per_device(): from_right = lax.ppermute(from_right, 'seq', downward)  14.6 us
    all_to_all x1, blocking collectives, per_device(): lax.all_to_all(partial_sums.astype(jnp.bfloat16), 'seq', split_axis=0, co...  13.4 us
    ppermute x3, starting transfers between devices, per_device(): from_right = lax.ppermute(from_right, 'seq', downward)  8.66 us
    all_gather x1, local copies, waits for them, and re-layouts, per_device(): gathered = lax.all_gather(local_context, 'seq', axis=0, tiled=True)  6.56 us
  transfers between devices with their start and end apart: 10, of which 8 were waited for; matrix products, arithmetic and copies ran while one was open for 5% of the time, Pallas kernels for 0%

profile of v1, /device:TPU:0, one launch (start us, length us, event | category | flops | bytes accessed | tf_op | source)
XLA Modules:
  0.0 233.0 jit_solution(5083613361332113164)
XLA Ops:
  6.5 2.1 copy.36
  8.7 1.3 copy.38
  10.5 2.9 %collective-permute-start.1 = (bf16[128,2048]{0,1:T(8,128)(2,1)S(1)}, bf16[128,2048]{0,1:T(8,128)(2,1)S(1)}, u32[]{:S(2)}, u32[]{:S(2)}) collective-permute-start(bf16[128,2048]{0,1:T(8,128)(2,1)S(1)} %copy.38), channel_id=1, source_target_pairs={{0,28},{4,0},{8,4},{12,8},{16,12},{20,16},{24,20},{28,24},{1,29},{... | collective-permute-start | bytes 1572872 | tf_op jit(solution)/shard_map/ppermute | solution.py:85
  13.5 9.8 %collective-permute-done = bf16[128,2048]{0,1:T(8,128)(2,1)S(1)} collective-permute-done((bf16[128,2048]{0,1:T(8,128)(2,1)S(1)}, bf16[128,2048]{0,1:T(8,128)(2,1)S(1)}, u32[]{:S(2)}, u32[]{:S(2)}) %collective-permute-start) | collective-permute-done | bytes 524320 | tf_op jit(solution)/shard_map/ppermute | solution.py:80
  23.2 4.2 %collective-permute-start.2 = (bf16[128,2048]{0,1:T(8,128)(2,1)S(1)}, bf16[128,2048]{0,1:T(8,128)(2,1)S(1)}, u32[]{:S(2)}, u32[]{:S(2)}) collective-permute-start(bf16[128,2048]{0,1:T(8,128)(2,1)S(1)} %collective-permute-done), channel_id=1, source_target_pairs={{0,4},{4,8},{8,12},{12,16},{16,20},{20,24},{24,28},{28,0},{1,5},{5... | collective-permute-start | bytes 1572872 | tf_op jit(solution)/shard_map/ppermute | solution.py:80
  27.4 3.0 %collective-permute-done.1 = bf16[128,2048]{0,1:T(8,128)(2,1)S(1)} collective-permute-done((bf16[128,2048]{0,1:T(8,128)(2,1)S(1)}, bf16[128,2048]{0,1:T(8,128)(2,1)S(1)}, u32[]{:S(2)}, u32[]{:S(2)}) %collective-permute-start.1) | collective-permute-done | bytes 524320 | tf_op jit(solution)/shard_map/ppermute | solution.py:85
  30.4 2.8 %collective-permute-start.3 = (bf16[128,2048]{0,1:T(8,128)(2,1)S(1)}, bf16[128,2048]{0,1:T(8,128)(2,1)}, u32[]{:S(2)}, u32[]{:S(2)}) collective-permute-start(bf16[128,2048]{0,1:T(8,128)(2,1)S(1)} %collective-permute-done.1), channel_id=1, source_target_pairs={{0,28},{4,0},{8,4},{12,8},{16,12},{20,16},{24,20},{28,24},{1,29},{... | collective-permute-start | bytes 1572872 | tf_op jit(solution)/shard_map/ppermute | solution.py:85
  33.2 2.5 %broadcast_in_dim.49 = bf16[1024,2048]{0,1:T(8,128)(2,1)} broadcast(bf16[]{:T(256)} %constant.127.clone.1), dimensions={} | broadcast | bytes 4194306 | tf_op jit(solution)/shard_map/broadcast_in_dim | solution.py:73
  35.8 0.9 constant_dynamic-update-slice_fusion.7
  37.3 0.9 collective-permute-done.2
  38.2 0.9 constant_dynamic-update-slice_fusion.6
  39.1 0.9 constant_dynamic-update-slice_fusion.5
  39.9 11.6 %collective-permute-done.3 = bf16[128,2048]{0,1:T(8,128)(2,1)} collective-permute-done((bf16[128,2048]{0,1:T(8,128)(2,1)S(1)}, bf16[128,2048]{0,1:T(8,128)(2,1)}, u32[]{:S(2)}, u32[]{:S(2)}) %collective-permute-start.3) | collective-permute-done | bytes 524320 | tf_op jit(solution)/shard_map/ppermute | solution.py:85
  51.5 2.9 %collective-permute-start.5 = (bf16[128,2048]{0,1:T(8,128)(2,1)}, bf16[128,2048]{0,1:T(8,128)(2,1)S(1)}, u32[]{:S(2)}, u32[]{:S(2)}) collective-permute-start(bf16[128,2048]{0,1:T(8,128)(2,1)} %collective-permute-done.3), channel_id=1, source_target_pairs={{0,28},{4,0},{8,4},{12,8},{16,12},{20,16},{24,20},{28,24},{1,29},{... | collective-permute-start | bytes 1572872 | tf_op jit(solution)/shard_map/ppermute | solution.py:85
  54.4 0.9 constant_dynamic-update-slice_fusion.4
  55.3 7.2 %collective-permute-done.4 = bf16[128,2048]{0,1:T(8,128)(2,1)S(1)} collective-permute-done((bf16[128,2048]{0,1:T(8,128)(2,1)S(1)}, bf16[128,2048]{0,1:T(8,128)(2,1)S(1)}, u32[]{:S(2)}, u32[]{:S(2)}) %collective-permute-start.4) | collective-permute-done | bytes 524320 | tf_op jit(solution)/shard_map/ppermute | solution.py:80
  62.5 1.9 constant_dynamic-update-slice_fusion.3
  64.5 0.9 constant_dynamic-update-slice_fusion.2
  65.4 0.9 constant_dynamic-update-slice_fusion.1
  66.3 5.7 %collective-permute-done.6 = bf16[128,2048]{0,1:T(8,128)(2,1)S(1)} collective-permute-done((bf16[128,2048]{0,1:T(8,128)(2,1)S(1)}, bf16[128,2048]{0,1:T(8,128)(2,1)S(1)}, u32[]{:S(2)}, u32[]{:S(2)}) %collective-permute-start.6) | collective-permute-done | bytes 524320 | tf_op jit(solution)/shard_map/ppermute | solution.py:80
  73.1 3.3 %while.19 = (s32[]{:T(128)}, f32[16,128]{1,0:T(8,128)S(1)}, f32[16,128]{1,0:T(8,128)S(1)}, f32[16,128,128]{2,1,0:T(8,128)S(1)}, s32[]{:T(128)}, /*index=5*/s32[]...) while((s32[]{:T(128)}, f32[16,128]{1,0:T(8,128)S(1)}, ...), condition=%wide.region_5.6_spmd, body=%wide.region_0.5_spmd.sunk | while | flops 137122048 | bytes 9111853 | solution.py:106
  73.1 3.0 %conditional.2 = ((f32[16,128]{1,0:T(8,128)S(1)}, f32[16,128]{1,0:T(8,128)S(1)}, f32[16,128,128]{2,1,0:T(8,128)S(1)})) conditional(s32[]{:T(128)} %convert_element_type.63, (f32[16,128]{1,0:T(8,128)S(1)}, f32[16,128]{1,0:T(8,128)S(1)}, f32[16,128,128]{2,1,0:T(8,128)S(1)}) %tuple.61, (s32[]{:T(128)}, s32[]{:T(128)}, bf16[1024,2048]{0,1:T(8,128)(2,1)}, ...), branch_computations={%region_1.1_spmd, %region_2.4_spmd} | conditional | flops 137122048 | bytes 9111630 | solution.py:44
  73.1 1.3 constant_dynamic-slice_fusion
  76.7 0.9 divide_convert_fusion
  77.8 57.0 %all-gather.5.cloned.1.call-done = bf16[1024,2048]{0,1:T(8,128)(2,1)} async-done(((bf16[128,2048]{0,1:T(8,128)(2,1)}), bf16[1024,2048]{0,1:T(8,128)(2,1)}) %all-gather.5.cloned.1.call-update) | async-done | bytes 4194320 | tf_op jit(solution)/shard_map/all_gather | solution.py:114
  134.7 6.6 %copy.43 = bf16[1024,2048]{1,0:T(8,128)(2,1)} copy(bf16[1024,2048]{0,1:T(8,128)(2,1)} %all-gather.5.cloned.1.call-done) | data formatting | bytes 8388608 | tf_op jit(solution)/shard_map/all_gather | solution.py:114
  141.3 2.7 %copy.44 = bf16[4,8,32,2048]{3,2,1,0:T(8,128)(2,1)S(1)} copy(bf16[4,8,32,2048]{3,2,0,1:T(8,128)(2,1)} %bitcast.29) | data formatting | bytes 8388608 | tf_op jit(solution)/shard_map/transpose | solution.py:118
  144.7 5.8 %convolution_convert_fusion = bf16[1024,1024]{1,0:T(8,128)(2,1)} fusion(bf16[1024,2048]{1,0:T(8,128)(2,1)S(1)} %bitcast.30, bf16[2048,1024]{1,0:T(8,128)(2,1)S(1)} %copy-done.2), kind=kOutput, calls=%fused_computation.18 | convolution fusion | flops 4296015872 | bytes 10485760 | tf_op jit(solution)/shard_map/dot_general | solution.py:120
  150.5 44.0 %reduce-scatter.2.cloned.1.call-done = bf16[256,1024]{1,0:T(8,128)(2,1)} async-done(((bf16[1024,1024]{1,0:T(8,128)(2,1)}), bf16[256,1024]{1,0:T(8,128)(2,1)}) %reduce-scatter.2.cloned.1.call-update) | async-done | bytes 524304 | tf_op jit(solution)/shard_map/reduce_scatter | solution.py:119
  194.5 13.4 %all_to_all.29 = bf16[8,32,1024]{2,1,0:T(8,128)(2,1)S(1)} all-to-all(bf16[8,32,1024]{2,1,0:T(8,128)(2,1)} %bitcast.34), channel_id=1, replica_groups=mesh['seq'=8,'chan'=4] {'seq'}, dimensions={0} | all-to-all | bytes 1048576 | tf_op jit(solution)/shard_map/all_to_all | solution.py:126
  208.9 16.7 %all_to_all.30 = bf16[32,4,2048]{2,0,1:T(8,128)(2,1)S(1)} all-to-all(bf16[32,4,2048]{2,0,1:T(8,128)(2,1)S(1)} %copy.46), channel_id=1, replica_groups=mesh['seq'=8,'chan'=4] {'chan'}, dimensions={1} | all-to-all | bytes 1048576 | tf_op jit(solution)/shard_map/all_to_all | solution.py:125
  225.6 0.9 fusion.9
  (42 shorter events, 6.0 us)
Async XLA Ops:
  6.5 30.1 %copy-start.1 = (bf16[128,2048]{1,0:T(8,128)(2,1)S(1)}, bf16[128,2048]{1,0:T(8,128)(2,1)}, u32[]{:S(2)}) copy-start(bf16[128,2048]{1,0:T(8,128)(2,1)} %param.9) | copy-start | bytes 1572868
  6.5 66.4 %all-gather.3.cloned.1.call-start = ((), (), s32[]{:S(2)}) async-start(), calls=%async_computation.3 | async-start | bytes 4718592 | tf_op jit(solution)/shard_map/all_gather | solution.py:69
  8.7 126.1 %all-gather.5.cloned.1.call-start = ((), (), s32[]{:S(2)}) async-start(), calls=%async_computation.4 | async-start | bytes 4718592 | tf_op jit(solution)/shard_map/all_gather | solution.py:114
  10.0 13.2 %collective-permute-start = (bf16[128,2048]{0,1:T(8,128)(2,1)S(1)}, bf16[128,2048]{0,1:T(8,128)(2,1)S(1)}, u32[]{:S(2)}, u32[]{:S(2)}) collective-permute-start(bf16[128,2048]{0,1:T(8,128)(2,1)S(1)} %copy.38), channel_id=1, source_target_pairs={{0,4},{4,8},{8,12},{12,16},{16,20},{20,24},{24,28},{28,0},{1,5},{5... | collective-permute-start | bytes 1572872 | tf_op jit(solution)/shard_map/ppermute | solution.py:80
  10.5 19.9 %collective-permute-start.1 = (bf16[128,2048]{0,1:T(8,128)(2,1)S(1)}, bf16[128,2048]{0,1:T(8,128)(2,1)S(1)}, u32[]{:S(2)}, u32[]{:S(2)}) collective-permute-start(bf16[128,2048]{0,1:T(8,128)(2,1)S(1)} %copy.38), channel_id=1, source_target_pairs={{0,28},{4,0},{8,4},{12,8},{16,12},{20,16},{24,20},{28,24},{1,29},{... | collective-permute-start | bytes 1572872 | tf_op jit(solution)/shard_map/ppermute | solution.py:85
  23.2 14.9 %collective-permute-start.2 = (bf16[128,2048]{0,1:T(8,128)(2,1)S(1)}, bf16[128,2048]{0,1:T(8,128)(2,1)S(1)}, u32[]{:S(2)}, u32[]{:S(2)}) collective-permute-start(bf16[128,2048]{0,1:T(8,128)(2,1)S(1)} %collective-permute-done), channel_id=1, source_target_pairs={{0,4},{4,8},{8,12},{12,16},{16,20},{20,24},{24,28},{28,0},{1,5},{5... | collective-permute-start | bytes 1572872 | tf_op jit(solution)/shard_map/ppermute | solution.py:80
  30.4 21.1 %collective-permute-start.3 = (bf16[128,2048]{0,1:T(8,128)(2,1)S(1)}, bf16[128,2048]{0,1:T(8,128)(2,1)}, u32[]{:S(2)}, u32[]{:S(2)}) collective-permute-start(bf16[128,2048]{0,1:T(8,128)(2,1)S(1)} %collective-permute-done.1), channel_id=1, source_target_pairs={{0,28},{4,0},{8,4},{12,8},{16,12},{20,16},{24,20},{28,24},{1,29},{... | collective-permute-start | bytes 1572872 | tf_op jit(solution)/shard_map/ppermute | solution.py:85
  38.2 24.4 %collective-permute-start.4 = (bf16[128,2048]{0,1:T(8,128)(2,1)S(1)}, bf16[128,2048]{0,1:T(8,128)(2,1)S(1)}, u32[]{:S(2)}, u32[]{:S(2)}) collective-permute-start(bf16[128,2048]{0,1:T(8,128)(2,1)S(1)} %collective-permute-done.2), channel_id=1, source_target_pairs={{0,4},{4,8},{8,12},{12,16},{16,20},{20,24},{24,28},{28,0},{1,5},{5... | collective-permute-start | bytes 1572872 | tf_op jit(solution)/shard_map/ppermute | solution.py:80
  51.5 13.9 %collective-permute-start.5 = (bf16[128,2048]{0,1:T(8,128)(2,1)}, bf16[128,2048]{0,1:T(8,128)(2,1)S(1)}, u32[]{:S(2)}, u32[]{:S(2)}) collective-permute-start(bf16[128,2048]{0,1:T(8,128)(2,1)} %collective-permute-done.3), channel_id=1, source_target_pairs={{0,28},{4,0},{8,4},{12,8},{16,12},{20,16},{24,20},{28,24},{1,29},{... | collective-permute-start | bytes 1572872 | tf_op jit(solution)/shard_map/ppermute | solution.py:85
  62.5 9.5 %collective-permute-start.6 = (bf16[128,2048]{0,1:T(8,128)(2,1)S(1)}, bf16[128,2048]{0,1:T(8,128)(2,1)S(1)}, u32[]{:S(2)}, u32[]{:S(2)}) collective-permute-start(bf16[128,2048]{0,1:T(8,128)(2,1)S(1)} %collective-permute-done.4), channel_id=1, source_target_pairs={{0,4},{4,8},{8,12},{12,16},{16,20},{20,24},{24,28},{28,0},{1,5},{5... | collective-permute-start | bytes 1572872 | tf_op jit(solution)/shard_map/ppermute | solution.py:80
  77.7 116.8 %reduce-scatter.2.cloned.1.call-start = ((), (), s32[]{:S(2)}) async-start(), calls=%async_computation.5 | async-start | bytes 2621440 | tf_op jit(solution)/shard_map/reduce_scatter | solution.py:119
  141.3 3.4 %copy-start.2 = (bf16[2048,1024]{1,0:T(8,128)(2,1)S(1)}, bf16[2048,1024]{1,0:T(8,128)(2,1)}, u32[]{:S(2)}) copy-start(bf16[2048,1024]{1,0:T(8,128)(2,1)} %param.13) | copy-start | bytes 12582916
  150.5 75.1 %copy-start = (bf16[128,2048]{1,0:T(8,128)(2,1)S(1)}, bf16[128,2048]{1,0:T(8,128)(2,1)}, u32[]{:S(2)}) copy-start(bf16[128,2048]{1,0:T(8,128)(2,1)} %param.12) | copy-start | bytes 1572868
Sparse Core Ops, SparseCore 0:
  9.2 52.8 all-gather.2
  77.8 56.8 all-gather.4
  150.6 43.8 reduce-scatter.1
